TPU v7x, 256 devices: a whole 4x4x8 slice. The times are simulated.
256 devices in a mesh: pipe: 8 (over z), seq: 32 (over y, x, core).
Axes of the slice: x: 4, y: 4, z: 8, core: 2. Of those that a mesh axis runs over, the one named last changes fastest.
Arguments:
- queries: bfloat16 [8, 4096, 8192], P('pipe', 'seq'), may hold values from -47.6 to 47.6
- keys: bfloat16 [8, 4096, 1024], P('pipe', 'seq'), may hold values from -4 to 4
- values: bfloat16 [8, 4096, 1024], P('pipe', 'seq'), may hold values from -6 to 6
- out_grad: bfloat16 [8, 4096, 8192], P('pipe', 'seq'), may hold values from -6 to 6
- window_blocks: int32 [64, 3], replicated, may hold values from 0 to 63, as said below
- global_blocks: int32 [64, 2], replicated, may hold values from 0 to 63, as said below
- random_blocks: int32 [64, 3], replicated, may hold values from 0 to 63
Outputs:
- handed_queries: bfloat16 [8, 4096, 8192], P('pipe', 'seq')
- handed_keys: bfloat16 [8, 4096, 1024], P('pipe', 'seq')
- handed_values: bfloat16 [8, 4096, 1024], P('pipe', 'seq')
Inputs may be any that keep to these rules, and one draw needn't show every extreme that they name: `window_blocks`: row b lists b - 1, b, b + 1; a neighbour that lies in another document of the pack, or outside the sequence, is replaced by b. `global_blocks`: every row lists the same two blocks: one below 64 // 2, and the last block 64 - 1.
All inputs are finite; a program needn't handle non-finite values.
Results may differ from a plain program's by a relative error of at most 0.012.
The roundings to bfloat16 on the way count: a program that leaves them out, or rounds other values in their place, can miss the bound.
Values may be sent and summed in bfloat16 or wider, within the bound.
No kernel may reach another device: no remote copies, remote signals or barrier semaphores. Data moves between devices by JAX's collectives and lax.ppermute only.
A program may use at most 128 MiB of HBM per device.

v0:
```python
import jax
import jax.numpy as jnp
from jax import lax
from jax.sharding import PartitionSpec as P

HEADS = 64
KV = 8
HD = 128
BLOCK = 64


def from_behind(block, axis, distance):
    devices = range(lax.axis_size(axis))
    route = [(i - distance, i) for i in devices if i - distance in devices]
    return lax.ppermute(block, axis, route)


def block_lists(window_blocks, global_blocks, random_blocks):
    listed = jnp.concatenate([window_blocks, global_blocks, random_blocks], axis=1)
    width = listed.shape[1]
    same = listed[:, :, None] == listed[:, None, :]
    earlier = jnp.arange(width)[None, :] < jnp.arange(width)[:, None]
    repeated = jnp.any(jnp.logical_and(same, earlier[None]), axis=2)
    return (listed, jnp.logical_not(repeated))


def block_grads(q_rows, g_rows, k_blocks, v_blocks, listed, live):
    count = listed.shape[0]
    slots = listed.shape[1]
    block = k_blocks.shape[1]
    depth = k_blocks.shape[2]
    scale = depth ** (-0.5)
    k_near = k_blocks[listed].reshape(count, slots * block, depth)
    v_near = v_blocks[listed].reshape(count, slots * block, depth)
    allowed = jnp.repeat(live, block, axis=1)[:, None, :]
    scores = jnp.einsum("grd,gsd->grs", q_rows, k_near, preferred_element_type=jnp.float32) * scale
    scores = jnp.where(allowed, scores, -jnp.inf)
    top = jnp.max(scores, axis=-1, keepdims=True)
    expd = jnp.exp(scores - top)
    probs = expd / jnp.sum(expd, axis=-1, keepdims=True)
    probs_low = probs.astype(jnp.bfloat16)
    attn_out = jnp.einsum(
        "grs,gsd->grd", probs_low, v_near, preferred_element_type=jnp.float32
    ).astype(jnp.bfloat16)
    attn_out = lax.optimization_barrier(attn_out)
    delta = jnp.sum(
        g_rows.astype(jnp.float32) * attn_out.astype(jnp.float32), axis=-1, keepdims=True
    )
    dprobs = jnp.einsum("grd,gsd->grs", g_rows, v_near, preferred_element_type=jnp.float32)
    ds_low = (probs * (dprobs - delta)).astype(jnp.bfloat16)
    grad_q = (
        jnp.einsum("grs,gsd->grd", ds_low, k_near, preferred_element_type=jnp.float32) * scale
    ).astype(jnp.bfloat16)
    dk_slots = (
        jnp.einsum("grs,grd->gsd", ds_low, q_rows, preferred_element_type=jnp.float32) * scale
    )
    dv_slots = jnp.einsum("grs,grd->gsd", probs_low, g_rows, preferred_element_type=jnp.float32)
    return (
        grad_q,
        dk_slots.reshape(count, slots, block, depth),
        dv_slots.reshape(count, slots, block, depth),
    )


def body(queries, keys, values, out_grad, window_blocks, global_blocks, random_blocks):
    lanes = lax.axis_size("seq")
    tok = queries.shape[1]
    repeat = lanes // KV
    q_local = queries[0].reshape(tok, HEADS, HD)
    g_local = out_grad[0].reshape(tok, HEADS, HD)
    q_heads, g_heads = (
        lax.all_to_all(q_local, "seq", split_axis=1, concat_axis=0, tiled=True),
        lax.all_to_all(g_local, "seq", split_axis=1, concat_axis=0, tiled=True),
    )
    k_all, v_all = (
        lax.all_gather(keys[0], "seq", axis=0, tiled=True),
        lax.all_gather(values[0], "seq", axis=0, tiled=True),
    )
    start = lax.axis_index("seq") // repeat * HD
    k_head = lax.dynamic_slice_in_dim(k_all, start, HD, 1)
    v_head = lax.dynamic_slice_in_dim(v_all, start, HD, 1)
    seqlen = q_heads.shape[0]
    per_device = q_heads.shape[1]
    nblocks = seqlen // BLOCK
    listed, live = block_lists(window_blocks, global_blocks, random_blocks)
    turns = 4
    span = nblocks // turns
    rows = BLOCK * per_device
    q_rows = q_heads.reshape(turns, span, rows, HD)
    g_rows = g_heads.reshape(turns, span, rows, HD)
    k_blocks = k_head.reshape(nblocks, BLOCK, HD)
    v_blocks = v_head.reshape(nblocks, BLOCK, HD)

    def step(carry, parts):
        dk_total, dv_total = carry
        q_part, g_part, list_part, live_part = parts
        grad_q, dk_slots, dv_slots = block_grads(
            q_part, g_part, k_blocks, v_blocks, list_part, live_part
        )
        return (
            (dk_total.at[list_part].add(dk_slots), dv_total.at[list_part].add(dv_slots)),
            grad_q,
        )

    zeros = jnp.zeros((nblocks, BLOCK, HD), jnp.float32)
    inputs = (q_rows, g_rows, listed.reshape(turns, span, -1), live.reshape(turns, span, -1))
    (dk_total, dv_total), grad_q = lax.scan(step, (zeros, zeros), inputs)
    dq_heads = grad_q.reshape(seqlen, per_device, HD)
    dq_tokens = lax.all_to_all(dq_heads, "seq", split_axis=0, concat_axis=1, tiled=True)
    dk_parts, dv_parts = (
        lax.all_to_all(
            dk_total.reshape(seqlen, 1, HD), "seq", split_axis=0, concat_axis=1, tiled=True
        ),
        lax.all_to_all(
            dv_total.reshape(seqlen, 1, HD), "seq", split_axis=0, concat_axis=1, tiled=True
        ),
    )
    dk_tokens = jnp.sum(dk_parts.reshape(tok, KV, repeat, HD), axis=2).astype(jnp.bfloat16)
    dv_tokens = jnp.sum(dv_parts.reshape(tok, KV, repeat, HD), axis=2).astype(jnp.bfloat16)
    dq_flat = dq_tokens.reshape(1, tok, HEADS * HD)
    dk_flat = dk_tokens.reshape(1, tok, KV * HD)
    dv_flat = dv_tokens.reshape(1, tok, KV * HD)
    return from_behind((dq_flat, dk_flat, dv_flat), "pipe", -1)


def solution(mesh):
    in_specs = (
        P("pipe", "seq", None),
        P("pipe", "seq", None),
        P("pipe", "seq", None),
        P("pipe", "seq", None),
        P(),
        P(),
        P(),
    )
    out_specs = (P("pipe", "seq", None), P("pipe", "seq", None), P("pipe", "seq", None))
    return jax.shard_map(body, mesh=mesh, in_specs=in_specs, out_specs=out_specs, check_vma=False)
```

profile of v0, /device:TPU:1, one launch (start us, length us, event | category | flops | bytes accessed | tf_op | source)
XLA Modules:
  0.0 614.2 jit_solution(1255116644743728596)
XLA Ops:
  8.6 4.1 copy.83
  12.7 8.6 %all-to-all-start = ((bf16[128,64,128]{0,2,1:T(8,128)(2,1)}), bf16[128,64,128]{0,2,1:T(8,128)(2,1)S(1)}, u32[]{:S(2)}, u32[]{:S(2)}) async-start(bf16[128,64,128]{0,2,1:T(8,128)(2,1)} %bitcast.124), calls=%async_computation | async-start | bytes 4194304 | tf_op jit(solution)/shard_map/all_to_all | solution.py:72
  21.3 4.1 copy.86
  25.4 27.1 %all-to-all-done = bf16[128,64,128]{0,2,1:T(8,128)(2,1)S(1)} async-done(((bf16[128,64,128]{0,2,1:T(8,128)(2,1)}), bf16[128,64,128]{0,2,1:T(8,128)(2,1)S(1)}, u32[]{:S(2)}, u32[]{:S(2)}) %all-to-all-start) | async-done | bytes 2097184 | tf_op jit(solution)/shard_map/all_to_all | solution.py:72
  52.5 6.8 %all-to-all-start.1 = ((bf16[128,64,128]{0,2,1:T(8,128)(2,1)}), bf16[128,64,128]{0,2,1:T(8,128)(2,1)}, u32[]{:S(2)}, u32[]{:S(2)}) async-start(bf16[128,64,128]{0,2,1:T(8,128)(2,1)} %bitcast.123), calls=%async_computation.1 | async-start | bytes 4194304 | tf_op jit(solution)/shard_map/all_to_all | solution.py:73
  59.6 3.8 copy.85
  63.4 37.7 %all-to-all-done.1 = bf16[128,64,128]{0,2,1:T(8,128)(2,1)} async-done(((bf16[128,64,128]{0,2,1:T(8,128)(2,1)}), bf16[128,64,128]{0,2,1:T(8,128)(2,1)}, u32[]{:S(2)}, u32[]{:S(2)}) %all-to-all-start.1) | async-done | bytes 2097184 | tf_op jit(solution)/shard_map/all_to_all | solution.py:73
  101.0 6.3 %copy.88 = bf16[32,128,2,128]{3,2,1,0:T(2,128)(2,1)} copy(bf16[32,128,2,128]{1,3,2,0:T(8,128)(2,1)} %bitcast.18) | data formatting | bytes 4194304 | tf_op jit(solution)/shard_map/all_to_all | solution.py:73
  108.6 57.6 %all-gather.7.cloned.1.call-done = bf16[1,4096,1024]{2,1,0:T(8,128)(2,1)} async-done(((bf16[1,128,1024]{2,1,0:T(8,128)(2,1)}), bf16[1,4096,1024]{2,1,0:T(8,128)(2,1)}) %all-gather.7.cloned.1.call-update) | async-done | bytes 8388624 | tf_op jit(solution)/shard_map/all_gather | solution.py:77
  171.7 292.9 %while.14 = (s32[]{:T(128)}, f32[64,64,128]{2,1,0:T(8,128)}, f32[64,64,128]{2,1,0:T(8,128)}, bf16[4,16,128,128]{3,2,1,0:T(8,128)(2,1)}, s32[4,16,8]{1,0,2:T(4,12...) while((s32[]{:T(128)}, f32[64,64,128]{2,1,0:T(8,128)}, ...), condition=%wide.region_7.8_spmd, body=%wide.region_1.7_spmd.sunk | while | flops 1628176256 | bytes 138499472 | solution.py:107
  172.9 4.1 fusion.63
  177.2 4.9 fusion.64
  184.1 3.4 gather_fusion
  193.0 4.2 convolution_multiply_fusion.3
  197.2 20.0 %scatter_fusion = f32[64,64,128]{2,1,0:T(8,128)} fusion(f32[64,64,128]{2,1,0:T(8,128)} %get-tuple-element.221, s32[128]{0:T(128)S(1)} %reshape.204, f32[128,64,128]{2,1,0:T(8,128)} %bitcast.110), kind=kCustom, calls=%fused_computation.2.clone.1 | custom fusion | flops 1048576 | bytes 12583424 | tf_op jit(solution)/shard_map/while/body/eval_jaxpr/scatter-add | solution.py:101
  217.2 3.7 fusion.67
  221.0 3.7 fusion.66
  224.7 20.3 %scatter_fusion.1 = f32[64,64,128]{2,1,0:T(8,128)} fusion(f32[64,64,128]{2,1,0:T(8,128)} %get-tuple-element.222, s32[128]{0:T(128)S(1)} %reshape.204, f32[128,64,128]{2,1,0:T(8,128)} %bitcast.109), kind=kCustom, calls=%fused_computation.3.clone.1 | custom fusion | flops 1048576 | bytes 12583424 | tf_op jit(solution)/shard_map/while/body/eval_jaxpr/scatter-add | solution.py:101
  246.1 4.1 fusion.63
  250.5 4.9 fusion.64
  266.3 4.2 convolution_multiply_fusion.3
  270.5 20.0 %scatter_fusion = f32[64,64,128]{2,1,0:T(8,128)} fusion(f32[64,64,128]{2,1,0:T(8,128)} %get-tuple-element.221, s32[128]{0:T(128)S(1)} %reshape.204, f32[128,64,128]{2,1,0:T(8,128)} %bitcast.110), kind=kCustom, calls=%fused_computation.2.clone.1 | custom fusion | flops 1048576 | bytes 12583424 | tf_op jit(solution)/shard_map/while/body/eval_jaxpr/scatter-add | solution.py:101
  290.5 3.7 fusion.67
  294.3 3.7 fusion.66
  298.0 20.1 %scatter_fusion.1 = f32[64,64,128]{2,1,0:T(8,128)} fusion(f32[64,64,128]{2,1,0:T(8,128)} %get-tuple-element.222, s32[128]{0:T(128)S(1)} %reshape.204, f32[128,64,128]{2,1,0:T(8,128)} %bitcast.109), kind=kCustom, calls=%fused_computation.3.clone.1 | custom fusion | flops 1048576 | bytes 12583424 | tf_op jit(solution)/shard_map/while/body/eval_jaxpr/scatter-add | solution.py:101
  319.3 4.1 fusion.63
  323.7 4.9 fusion.64
  330.5 3.4 gather_fusion
  339.5 4.2 convolution_multiply_fusion.3
  343.7 20.0 %scatter_fusion = f32[64,64,128]{2,1,0:T(8,128)} fusion(f32[64,64,128]{2,1,0:T(8,128)} %get-tuple-element.221, s32[128]{0:T(128)S(1)} %reshape.204, f32[128,64,128]{2,1,0:T(8,128)} %bitcast.110), kind=kCustom, calls=%fused_computation.2.clone.1 | custom fusion | flops 1048576 | bytes 12583424 | tf_op jit(solution)/shard_map/while/body/eval_jaxpr/scatter-add | solution.py:101
  363.7 3.7 fusion.67
  367.4 3.7 fusion.66
  371.2 20.2 %scatter_fusion.1 = f32[64,64,128]{2,1,0:T(8,128)} fusion(f32[64,64,128]{2,1,0:T(8,128)} %get-tuple-element.222, s32[128]{0:T(128)S(1)} %reshape.204, f32[128,64,128]{2,1,0:T(8,128)} %bitcast.109), kind=kCustom, calls=%fused_computation.3.clone.1 | custom fusion | flops 1048576 | bytes 12583424 | tf_op jit(solution)/shard_map/while/body/eval_jaxpr/scatter-add | solution.py:101
  392.5 4.1 fusion.63
  396.9 4.9 fusion.64
  412.7 4.2 convolution_multiply_fusion.3
  416.9 20.0 %scatter_fusion = f32[64,64,128]{2,1,0:T(8,128)} fusion(f32[64,64,128]{2,1,0:T(8,128)} %get-tuple-element.221, s32[128]{0:T(128)S(1)} %reshape.204, f32[128,64,128]{2,1,0:T(8,128)} %bitcast.110), kind=kCustom, calls=%fused_computation.2.clone.1 | custom fusion | flops 1048576 | bytes 12583424 | tf_op jit(solution)/shard_map/while/body/eval_jaxpr/scatter-add | solution.py:101
  436.9 3.7 fusion.67
  440.7 3.7 fusion.66
  444.4 20.2 %scatter_fusion.1 = f32[64,64,128]{2,1,0:T(8,128)} fusion(f32[64,64,128]{2,1,0:T(8,128)} %get-tuple-element.222, s32[128]{0:T(128)S(1)} %reshape.204, f32[128,64,128]{2,1,0:T(8,128)} %bitcast.109), kind=kCustom, calls=%fused_computation.3.clone.1 | custom fusion | flops 1048576 | bytes 12583424 | tf_op jit(solution)/shard_map/while/body/eval_jaxpr/scatter-add | solution.py:101
  464.6 34.0 %all_to_all.75 = bf16[4096,2,128]{2,1,0:T(2,128)(2,1)} all-to-all(bf16[4096,2,128]{2,1,0:T(2,128)(2,1)} %bitcast.126), channel_id=1, replica_groups=mesh['pipe'=8,'seq'=32] {'seq'}, dimensions={0} | all-to-all | bytes 4194304 | tf_op jit(solution)/shard_map/all_to_all | solution.py:109
  498.6 32.3 %all_to_all.76 = f32[4096,1,128]{2,1,0:T(1,128)} all-to-all(f32[4096,1,128]{2,1,0:T(1,128)S(1)} %bitcast.111), channel_id=1, replica_groups=mesh['pipe'=8,'seq'=32] {'seq'}, dimensions={0} | all-to-all | bytes 4194304 | tf_op jit(solution)/shard_map/all_to_all | solution.py:111
  530.9 4.1 all-to-all-start.4
  538.2 4.1 copy.92
  546.8 16.5 %all-to-all-done.4 = f32[4096,1,128]{2,1,0:T(1,128)S(1)} async-done(((f32[4096,1,128]{2,1,0:T(1,128)}), f32[4096,1,128]{2,1,0:T(1,128)S(1)}, u32[]{:S(2)}, u32[]{:S(2)}) %all-to-all-start.4) | async-done | bytes 2097184 | tf_op jit(solution)/shard_map/all_to_all | solution.py:114
  564.9 31.9 %collective-permute-done.1 = bf16[1,128,1024]{1,2,0:T(8,128)(2,1)S(1)} collective-permute-done((bf16[1,128,1024]{1,2,0:T(8,128)(2,1)S(1)}, bf16[1,128,1024]{1,2,0:T(8,128)(2,1)S(1)}, u32[]{:S(2)}, u32[]{:S(2)}) %collective-permute-start.1) | collective-permute-done | bytes 262176 | tf_op jit(solution)/shard_map/ppermute | solution.py:15
  597.7 4.8 collective-permute-done.2
  603.3 4.1 copy.95
  (134 shorter events, 61.8 us)
Async XLA Ops:
  7.2 100.2 %all-gather.5.cloned.1.call-start = ((), (), s32[]{:S(2)}) async-start(), calls=%async_computation.5 | async-start | bytes 8650752 | tf_op jit(solution)/shard_map/all_gather | solution.py:76
  7.9 158.3 %all-gather.7.cloned.1.call-start = ((), (), s32[]{:S(2)}) async-start(), calls=%async_computation.6 | async-start | bytes 8650752 | tf_op jit(solution)/shard_map/all_gather | solution.py:77
  12.7 39.8 %all-to-all-start = ((bf16[128,64,128]{0,2,1:T(8,128)(2,1)}), bf16[128,64,128]{0,2,1:T(8,128)(2,1)S(1)}, u32[]{:S(2)}, u32[]{:S(2)}) async-start(bf16[128,64,128]{0,2,1:T(8,128)(2,1)} %bitcast.124), calls=%async_computation | async-start | bytes 4194304 | tf_op jit(solution)/shard_map/all_to_all | solution.py:72
  52.5 6.8 %copy-start.6 = (s32[64,3]{0,1:T(4,128)S(1)}, s32[64,3]{0,1:T(4,128)}, u32[]{:S(2)}) copy-start(s32[64,3]{0,1:T(4,128)} %param.15) | copy-start | bytes 2308
  52.5 6.8 %copy-start.7 = (s32[64,3]{0,1:T(4,128)S(1)}, s32[64,3]{0,1:T(4,128)}, u32[]{:S(2)}) copy-start(s32[64,3]{0,1:T(4,128)} %param.13) | copy-start | bytes 2308
  52.5 6.8 %copy-start.8 = (s32[64,2]{0,1:T(2,128)S(1)}, s32[64,2]{0,1:T(2,128)}, u32[]{:S(2)}) copy-start(s32[64,2]{0,1:T(2,128)} %param.14) | copy-start | bytes 1540
  52.5 48.6 %all-to-all-start.1 = ((bf16[128,64,128]{0,2,1:T(8,128)(2,1)}), bf16[128,64,128]{0,2,1:T(8,128)(2,1)}, u32[]{:S(2)}, u32[]{:S(2)}) async-start(bf16[128,64,128]{0,2,1:T(8,128)(2,1)} %bitcast.123), calls=%async_computation.1 | async-start | bytes 4194304 | tf_op jit(solution)/shard_map/all_to_all | solution.py:73
  172.9 4.1 copy-start.1
  182.1 1.9 copy-start.3
  187.5 2.4 copy-start.5
  187.5 2.9 copy-start.2
  193.0 4.2 copy-start.4
  246.1 4.1 copy-start.1
  255.4 1.9 copy-start.3
  260.7 2.4 copy-start.5
  260.7 2.9 copy-start.2
  266.3 4.2 copy-start.4
  319.3 4.1 copy-start.1
  328.6 1.9 copy-start.3
  333.9 2.4 copy-start.5
  333.9 2.9 copy-start.2
  339.5 4.2 copy-start.4
  392.5 4.1 copy-start.1
  401.8 1.9 copy-start.3
  407.1 2.4 copy-start.5
  407.1 2.9 copy-start.2
  412.7 4.2 copy-start.4
  464.6 34.0 %copy-start = (f32[64,64,128]{2,1,0:T(8,128)S(1)}, f32[64,64,128]{2,1,0:T(8,128)}, u32[]{:S(2)}) copy-start(f32[64,64,128]{2,1,0:T(8,128)} %get-tuple-element.58) | copy-start | bytes 6291460
  530.9 32.4 %all-to-all-start.4 = ((f32[4096,1,128]{2,1,0:T(1,128)}), f32[4096,1,128]{2,1,0:T(1,128)S(1)}, u32[]{:S(2)}, u32[]{:S(2)}) async-start(f32[4096,1,128]{2,1,0:T(1,128)} %bitcast.30), calls=%async_computation.4 | async-start | bytes 4194304 | tf_op jit(solution)/shard_map/all_to_all | solution.py:114
  542.3 61.0 %collective-permute-start = (bf16[1,128,8192]{1,2,0:T(8,128)(2,1)}, bf16[1,128,8192]{1,2,0:T(8,128)(2,1)}, u32[]{:S(2)}, u32[]{:S(2)}) collective-permute-start(bf16[1,128,8192]{1,2,0:T(8,128)(2,1)} %bitcast.127), channel_id=1, source_target_pairs={{32,0},{64,32},{96,64},{128,96},{160,128},{192,160},{224,192},{33,... | collective-permute-start | bytes 6291464 | tf_op jit(solution)/shard_map/ppermute | solution.py:15
  545.5 51.3 %collective-permute-start.1 = (bf16[1,128,1024]{1,2,0:T(8,128)(2,1)S(1)}, bf16[1,128,1024]{1,2,0:T(8,128)(2,1)S(1)}, u32[]{:S(2)}, u32[]{:S(2)}) collective-permute-start(bf16[1,128,1024]{1,2,0:T(8,128)(2,1)S(1)} %bitcast.129), channel_id=1, source_target_pairs={{32,0},{64,32},{96,64},{128,96},{160,128},{192,160},{224,192},{33,... | collective-permute-start | bytes 786440 | tf_op jit(solution)/shard_map/ppermute | solution.py:15
  563.6 38.8 %collective-permute-start.2 = (bf16[1,128,1024]{1,2,0:T(8,128)(2,1)S(1)}, bf16[1,128,1024]{1,2,0:T(8,128)(2,1)S(1)}, u32[]{:S(2)}, u32[]{:S(2)}) collective-permute-start(bf16[1,128,1024]{1,2,0:T(8,128)(2,1)S(1)} %bitcast.130), channel_id=1, source_target_pairs={{32,0},{64,32},{96,64},{128,96},{160,128},{192,160},{224,192},{33,... | collective-permute-start | bytes 786440 | tf_op jit(solution)/shard_map/ppermute | solution.py:15
Sparse Core Ops, SparseCore 0:
  10.5 93.9 all-gather.4
  107.1 59.0 all-gather.6
where the time goes:
time: 618 us; the launch traced here: 614 us
  other arithmetic  185 us (30%)
  waiting for transfers between devices  177 us (29%)
  matrix products  83.6 us (14%)
  blocking collectives  66.3 us (11%)
  local copies, waits for them, and re-layouts  64 us (10%)
  starting transfers between devices  23.3 us (4%)
  between operations  14.2 us (2%)
    scatter-add x4, other arithmetic, step(): dv_total.at[list_part].add(dv_slots)  80.8 us
    scatter-add x4, other arithmetic, step(): dk_total.at[list_part].add(dk_slots)  80.1 us
    all_gather x1, waiting for transfers between devices, body(): lax.all_gather(values[0], 'seq', axis=0, tiled=True)  57.6 us
    all_to_all x1, waiting for transfers between devices, body(): lax.all_to_all(g_local, 'seq', split_axis=1, concat_axis=0, tiled=True)  37.7 us
    ppermute x3, waiting for transfers between devices, from_behind(): return lax.ppermute(block, axis, route)  36.7 us
    all_to_all x1, blocking collectives, body(): lax.all_to_all(dq_heads, 'seq', split_axis=0, concat_axis=1, tiled=True)  34 us
    all_to_all x1, blocking collectives, body(): lax.all_to_all(dk_total.reshape(seqlen, 1, HD), 'seq', split_axis=0, conc...  32.3 us
    all_to_all x1, waiting for transfers between devices, body(): lax.all_to_all(q_local, 'seq', split_axis=1, concat_axis=0, tiled=True)  27.1 us
  transfers between devices with their start and end apart: 8, of which 6 were waited for; matrix products, arithmetic and copies ran while one was open for 5% of the time, Pallas kernels for 0%

commit v1 on v0

--- a/solution.py
+++ b/solution.py
@@ -7,6 +7,15 @@
 KV = 8
 HD = 128
 BLOCK = 64
+
+
+def shape_slots(a0, axis_id):
+    return jnp.concatenate(
+        lax.all_to_all(
+            jnp.stack(lax.axis_size(axis_id) * [a0]), concat_axis=0, axis_name=axis_id, split_axis=0
+        ),
+        axis=0,
+    )
 
 
 def from_behind(block, axis, distance):
@@ -74,7 +83,7 @@
     )
     k_all, v_all = (
         lax.all_gather(keys[0], "seq", axis=0, tiled=True),
-        lax.all_gather(values[0], "seq", axis=0, tiled=True),
+        shape_slots(values[0], "seq"),
     )
     start = lax.axis_index("seq") // repeat * HD
     k_head = lax.dynamic_slice_in_dim(k_all, start, HD, 1)

time: 618 us -> 673 us (1.089)
  blocking collectives: 66.3 us -> 121 us
    all_gather x1 -> x0, waiting for transfers between devices: 57.6 us -> none  [body(): lax.all_gather(values[0], 'seq', axis=0, tiled=True)]
    all_to_all x1, waiting for transfers between devices: 37.7 us -> 90 us  [shape_slots(): lax.all_to_all(jnp.stack(lax.axis_size(axis_id) * [a0]), concat_axis=0, a...]
    all_to_all x0 -> x1, blocking collectives: none -> 50.1 us  [body(): lax.all_to_all(g_local, 'seq', split_axis=1, concat_axis=0, tiled=True)]
    unnamed x13 -> x15, local copies, waits for them, and re-layouts: 13.9 us -> 13.9 us
  transfers between devices with their start and end apart: 8 -> 7, of which waited for: 6 -> 5; matrix products, arithmetic and copies ran while one was open for 5% -> 5% of each run, Pallas kernels for 0% -> 0%
where the time goes in v1:
time: 673 us; the launch traced here: 668 us
  other arithmetic  186 us (28%)
  waiting for transfers between devices  173 us (26%)
  blocking collectives  121 us (18%)
  matrix products  83.6 us (12%)
  local copies, waits for them, and re-layouts  68.3 us (10%)
  starting transfers between devices  22.2 us (3%)
  between operations  14.2 us (2%)
    all_to_all x1, waiting for transfers between devices, shape_slots(): lax.all_to_all(jnp.stack(lax.axis_size(axis_id) * [a0]), concat_axis=0, a...  90 us
    scatter-add x4, other arithmetic, step(): dv_total.at[list_part].add(dv_slots)  81 us
    scatter-add x4, other arithmetic, step(): dk_total.at[list_part].add(dk_slots)  80.1 us
    all_to_all x1, blocking collectives, body(): lax.all_to_all(g_local, 'seq', split_axis=1, concat_axis=0, tiled=True)  50.1 us
    all_to_all x1, blocking collectives, body(): lax.all_to_all(dq_heads, 'seq', split_axis=0, concat_axis=1, tiled=True)  38.6 us
    ppermute x3, waiting for transfers between devices, from_behind(): return lax.ppermute(block, axis, route)  38.2 us
    all_to_all x1, blocking collectives, body(): lax.all_to_all(dk_total.reshape(seqlen, 1, HD), 'seq', split_axis=0, conc...  32.1 us
    all_to_all x1, waiting for transfers between devices, body(): lax.all_to_all(q_local, 'seq', split_axis=1, concat_axis=0, tiled=True)  27.1 us
  transfers between devices with their start and end apart: 7, of which 5 were waited for; matrix products, arithmetic and copies ran while one was open for 5% of the time, Pallas kernels for 0%

profile of v1, /device:TPU:1, one launch (start us, length us, event | category | flops | bytes accessed | tf_op | source)
XLA Modules:
  0.0 667.9 jit_solution(11795916260994194285)
XLA Ops:
  7.9 4.1 copy.83
  12.0 8.6 %all-to-all-start = ((bf16[128,64,128]{0,2,1:T(8,128)(2,1)}), bf16[128,64,128]{0,2,1:T(8,128)(2,1)S(1)}, u32[]{:S(2)}, u32[]{:S(2)}) async-start(bf16[128,64,128]{0,2,1:T(8,128)(2,1)} %bitcast.126), calls=%async_computation | async-start | bytes 4194304 | tf_op jit(solution)/shard_map/all_to_all | solution.py:81
  20.6 4.1 copy.86
  24.6 27.1 %all-to-all-done = bf16[128,64,128]{0,2,1:T(8,128)(2,1)S(1)} async-done(((bf16[128,64,128]{0,2,1:T(8,128)(2,1)}), bf16[128,64,128]{0,2,1:T(8,128)(2,1)S(1)}, u32[]{:S(2)}, u32[]{:S(2)}) %all-to-all-start) | async-done | bytes 2097184 | tf_op jit(solution)/shard_map/all_to_all | solution.py:81
  51.8 50.1 %all_to_all.80 = bf16[128,64,128]{0,2,1:T(8,128)(2,1)} all-to-all(bf16[128,64,128]{0,2,1:T(8,128)(2,1)} %bitcast.127), channel_id=1, replica_groups=mesh['pipe'=8,'seq'=32] {'seq'}, dimensions={1} | all-to-all | bytes 4194304 | tf_op jit(solution)/shard_map/all_to_all | solution.py:82
  101.9 4.3 stack.3
  106.2 5.7 all-to-all-start.2
  112.3 3.8 copy.85
  116.1 6.2 copy.88
  122.3 90.0 %all-to-all-done.2 = bf16[32,128,1024]{2,1,0:T(8,128)(2,1)} async-done(((bf16[32,128,1024]{2,1,0:T(8,128)(2,1)}), bf16[32,128,1024]{2,1,0:T(8,128)(2,1)}, u32[]{:S(2)}, u32[]{:S(2)}) %all-to-all-start.2) | async-done | bytes 8388640 | tf_op jit(solution)/shard_map/all_to_all | solution.py:14
  219.2 293.2 %while.14 = (s32[]{:T(128)}, f32[64,64,128]{2,1,0:T(8,128)}, f32[64,64,128]{2,1,0:T(8,128)}, bf16[4,16,128,128]{3,2,1,0:T(8,128)(2,1)}, s32[4,16,8]{1,0,2:T(4,12...) while((s32[]{:T(128)}, f32[64,64,128]{2,1,0:T(8,128)}, ...), condition=%wide.region_7.8_spmd, body=%wide.region_1.7_spmd.sunk | while | flops 1628176256 | bytes 138499472 | solution.py:116
  221.6 4.1 fusion.63
  225.9 4.9 fusion.64
  240.5 4.2 convolution_multiply_fusion.3
  244.7 20.0 %scatter_fusion = f32[64,64,128]{2,1,0:T(8,128)} fusion(f32[64,64,128]{2,1,0:T(8,128)} %get-tuple-element.221, s32[128]{0:T(128)S(1)} %reshape.206, f32[128,64,128]{2,1,0:T(8,128)} %bitcast.112), kind=kCustom, calls=%fused_computation.2.clone.1 | custom fusion | flops 1048576 | bytes 12583424 | tf_op jit(solution)/shard_map/while/body/eval_jaxpr/scatter-add | solution.py:110
  264.7 3.8 fusion.67
  268.5 3.8 fusion.66
  272.2 20.3 %scatter_fusion.1 = f32[64,64,128]{2,1,0:T(8,128)} fusion(f32[64,64,128]{2,1,0:T(8,128)} %get-tuple-element.222, s32[128]{0:T(128)S(1)} %reshape.206, f32[128,64,128]{2,1,0:T(8,128)} %bitcast.111), kind=kCustom, calls=%fused_computation.3.clone.1 | custom fusion | flops 1048576 | bytes 12583424 | tf_op jit(solution)/shard_map/while/body/eval_jaxpr/scatter-add | solution.py:110
  294.9 4.1 fusion.63
  299.3 4.9 fusion.64
  313.8 4.2 convolution_multiply_fusion.3
  318.0 20.0 %scatter_fusion = f32[64,64,128]{2,1,0:T(8,128)} fusion(f32[64,64,128]{2,1,0:T(8,128)} %get-tuple-element.221, s32[128]{0:T(128)S(1)} %reshape.206, f32[128,64,128]{2,1,0:T(8,128)} %bitcast.112), kind=kCustom, calls=%fused_computation.2.clone.1 | custom fusion | flops 1048576 | bytes 12583424 | tf_op jit(solution)/shard_map/while/body/eval_jaxpr/scatter-add | solution.py:110
  338.1 3.8 fusion.67
  341.8 3.8 fusion.66
  345.6 20.4 %scatter_fusion.1 = f32[64,64,128]{2,1,0:T(8,128)} fusion(f32[64,64,128]{2,1,0:T(8,128)} %get-tuple-element.222, s32[128]{0:T(128)S(1)} %reshape.206, f32[128,64,128]{2,1,0:T(8,128)} %bitcast.111), kind=kCustom, calls=%fused_computation.3.clone.1 | custom fusion | flops 1048576 | bytes 12583424 | tf_op jit(solution)/shard_map/while/body/eval_jaxpr/scatter-add | solution.py:110
  368.3 4.1 fusion.63
  372.7 4.9 fusion.64
  387.3 4.2 convolution_multiply_fusion.3
  391.5 20.0 %scatter_fusion = f32[64,64,128]{2,1,0:T(8,128)} fusion(f32[64,64,128]{2,1,0:T(8,128)} %get-tuple-element.221, s32[128]{0:T(128)S(1)} %reshape.206, f32[128,64,128]{2,1,0:T(8,128)} %bitcast.112), kind=kCustom, calls=%fused_computation.2.clone.1 | custom fusion | flops 1048576 | bytes 12583424 | tf_op jit(solution)/shard_map/while/body/eval_jaxpr/scatter-add | solution.py:110
  411.5 3.7 fusion.67
  415.2 3.8 fusion.66
  419.0 20.2 %scatter_fusion.1 = f32[64,64,128]{2,1,0:T(8,128)} fusion(f32[64,64,128]{2,1,0:T(8,128)} %get-tuple-element.222, s32[128]{0:T(128)S(1)} %reshape.206, f32[128,64,128]{2,1,0:T(8,128)} %bitcast.111), kind=kCustom, calls=%fused_computation.3.clone.1 | custom fusion | flops 1048576 | bytes 12583424 | tf_op jit(solution)/shard_map/while/body/eval_jaxpr/scatter-add | solution.py:110
  441.5 4.1 fusion.63
  445.9 4.9 fusion.64
  460.5 4.2 convolution_multiply_fusion.3
  464.7 20.0 %scatter_fusion = f32[64,64,128]{2,1,0:T(8,128)} fusion(f32[64,64,128]{2,1,0:T(8,128)} %get-tuple-element.221, s32[128]{0:T(128)S(1)} %reshape.206, f32[128,64,128]{2,1,0:T(8,128)} %bitcast.112), kind=kCustom, calls=%fused_computation.2.clone.1 | custom fusion | flops 1048576 | bytes 12583424 | tf_op jit(solution)/shard_map/while/body/eval_jaxpr/scatter-add | solution.py:110
  484.7 3.7 fusion.67
  488.4 3.8 fusion.66
  492.2 20.2 %scatter_fusion.1 = f32[64,64,128]{2,1,0:T(8,128)} fusion(f32[64,64,128]{2,1,0:T(8,128)} %get-tuple-element.222, s32[128]{0:T(128)S(1)} %reshape.206, f32[128,64,128]{2,1,0:T(8,128)} %bitcast.111), kind=kCustom, calls=%fused_computation.3.clone.1 | custom fusion | flops 1048576 | bytes 12583424 | tf_op jit(solution)/shard_map/while/body/eval_jaxpr/scatter-add | solution.py:110
  512.4 38.6 %all_to_all.81 = bf16[4096,2,128]{2,1,0:T(2,128)(2,1)} all-to-all(bf16[4096,2,128]{2,1,0:T(2,128)(2,1)} %bitcast.129), channel_id=1, replica_groups=mesh['pipe'=8,'seq'=32] {'seq'}, dimensions={0} | all-to-all | bytes 4194304 | tf_op jit(solution)/shard_map/all_to_all | solution.py:118
  551.0 32.1 %all_to_all.82 = f32[4096,1,128]{2,1,0:T(1,128)} all-to-all(f32[4096,1,128]{2,1,0:T(1,128)S(1)} %bitcast.113), channel_id=1, replica_groups=mesh['pipe'=8,'seq'=32] {'seq'}, dimensions={0} | all-to-all | bytes 4194304 | tf_op jit(solution)/shard_map/all_to_all | solution.py:120
  583.1 4.1 all-to-all-start.5
  587.2 3.2 copy.91
  590.4 4.1 copy.92
  599.0 16.5 %all-to-all-done.5 = f32[4096,1,128]{2,1,0:T(1,128)S(1)} async-done(((f32[4096,1,128]{2,1,0:T(1,128)}), f32[4096,1,128]{2,1,0:T(1,128)S(1)}, u32[]{:S(2)}, u32[]{:S(2)}) %all-to-all-start.5) | async-done | bytes 2097184 | tf_op jit(solution)/shard_map/all_to_all | solution.py:123
  617.1 33.4 %collective-permute-done.1 = bf16[1,128,1024]{1,2,0:T(8,128)(2,1)S(1)} collective-permute-done((bf16[1,128,1024]{1,2,0:T(8,128)(2,1)S(1)}, bf16[1,128,1024]{1,2,0:T(8,128)(2,1)S(1)}, u32[]{:S(2)}, u32[]{:S(2)}) %collective-permute-start.1) | collective-permute-done | bytes 262176 | tf_op jit(solution)/shard_map/ppermute | solution.py:24
  651.4 4.8 collective-permute-done.2
  657.0 4.1 copy.95
  (135 shorter events, 64.7 us)
Async XLA Ops:
  7.2 206.5 %all-gather.3.cloned.1.call-start = ((), (), s32[]{:S(2)}) async-start(), calls=%async_computation.6 | async-start | bytes 8650752 | tf_op jit(solution)/shard_map/all_gather | solution.py:85
  12.0 39.8 %all-to-all-start = ((bf16[128,64,128]{0,2,1:T(8,128)(2,1)}), bf16[128,64,128]{0,2,1:T(8,128)(2,1)S(1)}, u32[]{:S(2)}, u32[]{:S(2)}) async-start(bf16[128,64,128]{0,2,1:T(8,128)(2,1)} %bitcast.126), calls=%async_computation | async-start | bytes 4194304 | tf_op jit(solution)/shard_map/all_to_all | solution.py:81
  51.8 50.1 %copy-start.6 = (bf16[1,128,1024]{2,1,0:T(8,128)(2,1)S(1)}, bf16[1,128,1024]{2,1,0:T(8,128)(2,1)}, u32[]{:S(2)}) copy-start(bf16[1,128,1024]{2,1,0:T(8,128)(2,1)} %param.11) | copy-start | bytes 786436
  106.2 5.8 copy-start.7
  106.2 5.8 copy-start.8
  106.2 5.8 copy-start.9
  106.2 106.2 %all-to-all-start.2 = ((bf16[32,128,1024]{2,1,0:T(8,128)(2,1)}), bf16[32,128,1024]{2,1,0:T(8,128)(2,1)}, u32[]{:S(2)}, u32[]{:S(2)}) async-start(bf16[32,128,1024]{2,1,0:T(8,128)(2,1)} %stack.3), calls=%async_computation.2 | async-start | bytes 16777216 | tf_op jit(solution)/shard_map/all_to_all | solution.py:14
  221.6 4.1 copy-start.1
  230.8 1.9 copy-start.3
  234.9 2.4 copy-start.5
  234.9 2.9 copy-start.2
  240.5 4.2 copy-start.4
  294.9 4.1 copy-start.1
  304.2 1.9 copy-start.3
  308.3 2.4 copy-start.5
  308.3 2.9 copy-start.2
  313.8 4.2 copy-start.4
  368.3 4.1 copy-start.1
  377.6 1.9 copy-start.3
  381.7 2.4 copy-start.5
  381.7 2.9 copy-start.2
  387.3 4.2 copy-start.4
  441.5 4.1 copy-start.1
  450.8 1.9 copy-start.3
  454.9 2.4 copy-start.5
  454.9 2.9 copy-start.2
  460.5 4.2 copy-start.4
  512.4 38.6 %copy-start = (f32[64,64,128]{2,1,0:T(8,128)S(1)}, f32[64,64,128]{2,1,0:T(8,128)}, u32[]{:S(2)}) copy-start(f32[64,64,128]{2,1,0:T(8,128)} %get-tuple-element.58) | copy-start | bytes 6291460
  583.1 32.4 %all-to-all-start.5 = ((f32[4096,1,128]{2,1,0:T(1,128)}), f32[4096,1,128]{2,1,0:T(1,128)S(1)}, u32[]{:S(2)}, u32[]{:S(2)}) async-start(f32[4096,1,128]{2,1,0:T(1,128)} %bitcast.32), calls=%async_computation.5 | async-start | bytes 4194304 | tf_op jit(solution)/shard_map/all_to_all | solution.py:123
  594.5 62.5 %collective-permute-start = (bf16[1,128,8192]{1,2,0:T(8,128)(2,1)}, bf16[1,128,8192]{1,2,0:T(8,128)(2,1)}, u32[]{:S(2)}, u32[]{:S(2)}) collective-permute-start(bf16[1,128,8192]{1,2,0:T(8,128)(2,1)} %bitcast.130), channel_id=1, source_target_pairs={{32,0},{64,32},{96,64},{128,96},{160,128},{192,160},{224,192},{33,... | collective-permute-start | bytes 6291464 | tf_op jit(solution)/shard_map/ppermute | solution.py:24
  597.7 52.8 %collective-permute-start.1 = (bf16[1,128,1024]{1,2,0:T(8,128)(2,1)S(1)}, bf16[1,128,1024]{1,2,0:T(8,128)(2,1)S(1)}, u32[]{:S(2)}, u32[]{:S(2)}) collective-permute-start(bf16[1,128,1024]{1,2,0:T(8,128)(2,1)S(1)} %bitcast.133), channel_id=1, source_target_pairs={{32,0},{64,32},{96,64},{128,96},{160,128},{192,160},{224,192},{33,... | collective-permute-start | bytes 786440 | tf_op jit(solution)/shard_map/ppermute | solution.py:24
  615.8 40.3 %collective-permute-start.2 = (bf16[1,128,1024]{1,2,0:T(8,128)(2,1)S(1)}, bf16[1,128,1024]{1,2,0:T(8,128)(2,1)S(1)}, u32[]{:S(2)}, u32[]{:S(2)}) collective-permute-start(bf16[1,128,1024]{1,2,0:T(8,128)(2,1)S(1)} %bitcast.134), channel_id=1, source_target_pairs={{32,0},{64,32},{96,64},{128,96},{160,128},{192,160},{224,192},{33,... | collective-permute-start | bytes 786440 | tf_op jit(solution)/shard_map/ppermute | solution.py:24
Sparse Core Ops, SparseCore 0:
  10.5 92.8 all-gather.2
